TPU v7x, 128 devices: a whole 4x4x4 slice. The times are simulated.
128 devices in a mesh: row: 16 (over z_lo, x, core), col: 8 (over y, z_hi).
Axes of the slice: x: 4, y: 4, z: 4 (z_hi: 2, z_lo: 2; z = z_hi * 2 + z_lo), core: 2. Of those that a mesh axis runs over, the one named last changes fastest.
Arguments:
- shared_rows: float32 [2048, 16384], P('row', 'col'), may hold values from -0.125 to 0.125
- event_counts: int32 [16], replicated, may hold values from 32 to 128, as said below
- ridge: float32 [16384], P('col'), may hold values from 0.5 to 2
- items: float32 [1024, 16384], P('row', 'col'), may hold values from -6 to 6
- cand_ids: int32 [512], replicated, may hold values from 0 to 1023
- theta: float32 [16384], P('col'), may hold values from -0.046875 to 0.046875
Outputs:
- gram_tile: float32 [16384, 16384], P('row', 'col')
- scores: float32 [512], replicated
Inputs may be any that keep to these rules, and one draw needn't show every extreme that they name: event_counts[s] counts the live slots at the start of row shard s's 128 slots; some shard is full.
All inputs are finite; a program needn't handle non-finite values.
Results may differ from a plain program's by a relative error of at most 0.000068.
Values sent between devices are 32-bit elements; how exact they have to be, the bound alone decides.
No kernel may reach another device: no remote copies, remote signals or barrier semaphores. Data moves between devices by JAX's collectives and lax.ppermute only.
A program may use at most 128 MiB of HBM per device.

v0:
```python
import jax
import jax.numpy as jnp
from jax import lax
from jax.sharding import Mesh
from jax.sharding import PartitionSpec as P

F = 16384
highest = lax.Precision.HIGHEST
high = lax.Precision.HIGH
ROW = ("zl", "x", "core")
COL = ("y", "zh")


def body(shared_rows, event_counts, ridge, items, cand_ids, theta):
    n_row = lax.axis_size("zl") * lax.axis_size("x") * lax.axis_size("core")
    n_col = lax.axis_size("y") * lax.axis_size("zh")
    ratio = n_row // n_col
    row_pos = (lax.axis_index("zl") * lax.axis_size("x") + lax.axis_index("x")) * lax.axis_size(
        "core"
    ) + lax.axis_index("core")
    col_pos = lax.axis_index("y") * lax.axis_size("zh") + lax.axis_index("zh")
    ev_slots, width_col = shared_rows.shape
    width_row = width_col // ratio
    slot = lax.iota(jnp.int32, ev_slots)
    masked = jnp.where((slot < event_counts[row_pos])[:, None], shared_rows, jnp.float32(0.0))
    col_all = masked
    for name in reversed(ROW):
        col_all = lax.all_gather(col_all, name, axis=0, tiled=True)
    halves = masked.reshape(ev_slots, ratio, width_row)
    received = []
    for t in range(ratio):
        perm = []
        for s in range(n_row):
            for c in range(n_col):
                b = s % ratio ^ t
                perm.append((s * n_col + c, (ratio * c + b) * n_col + s // ratio))
        piece = halves[:, row_pos % ratio ^ t, :]
        received.append(lax.ppermute(piece, ROW + COL, perm))
    parity = row_pos % ratio
    ordered = [
        sum((jnp.where(parity ^ t == a, received[t], 0.0) for t in range(ratio)))
        for a in range(ratio)
    ]
    row_block = jnp.concatenate(ordered, axis=0)
    row_all = row_block
    for name in reversed(COL):
        row_all = lax.all_gather(row_all, name, axis=0, tiled=True)
    contract = (((0,), (0,)), ((), ()))
    tile = lax.dot_general(
        row_all, col_all, contract, precision=high, preferred_element_type=jnp.float32
    )
    rows_global = row_pos * width_row + lax.broadcasted_iota(jnp.int32, (width_row, width_col), 0)
    cols_global = col_pos * width_col + lax.broadcasted_iota(jnp.int32, (width_row, width_col), 1)
    tile = tile + jnp.where(rows_global == cols_global, ridge[None, :], jnp.float32(0.0))
    z_part = lax.dot_general(
        col_all, items, (((1,), (1,)), ((), ())), precision=high, preferred_element_type=jnp.float32
    )
    q_ridge = jnp.sum(ridge[None, :] * items * items, axis=1)
    lin = jnp.dot(items, theta, precision=highest, preferred_element_type=jnp.float32)
    packed = jnp.concatenate([z_part, q_ridge[None, :], lin[None, :]], axis=0)
    step = n_col // 2
    while step >= 1:
        pairs = [(c, c ^ step) for c in range(n_col)]
        packed = packed + lax.ppermute(packed, COL, pairs)
        step //= 2
    ev_all = z_part.shape[0]
    z = packed[:ev_all]
    quad = jnp.sum(z * z, axis=0) + packed[ev_all]
    item_scores = packed[ev_all + 1] + jnp.sqrt(quad / F)
    items_dev = items.shape[0]
    held = item_scores
    step = 1
    while step < n_row:
        pairs = [(r, r ^ step) for r in range(n_row)]
        other = lax.ppermute(held, ROW, pairs)
        low = row_pos & step == 0
        held = jnp.where(low, jnp.concatenate([held, other]), jnp.concatenate([other, held]))
        step *= 2
    scores = held[cand_ids]
    return (tile, scores)


def solution(mesh):
    n_row = mesh.shape["row"]
    n_col = mesh.shape["col"]
    inner = Mesh(mesh.devices.reshape(2, n_row // 4, 2, n_col // 2, 2), ROW + COL)
    return jax.shard_map(
        body,
        mesh=inner,
        in_specs=(P(ROW, COL), P(), P(COL), P(ROW, COL), P(), P(COL)),
        out_specs=(P(ROW, COL), P()),
        check_vma=False,
    )
```

profile of v0, /device:TPU:1, one launch (start us, length us, event | category | flops | bytes accessed | tf_op | source)
XLA Modules:
  0.0 542.4 jit_solution(11801109031130123210)
XLA Ops:
  7.2 0.0 copy-start
  7.2 0.0 all-gather.10.cloned.1.call-start
  7.2 1.2 dynamic_slice.9
  8.5 0.6 iota_compare_fusion
  9.1 2.3 broadcast_select_fusion
  11.5 0.0 all-gather.10.cloned.1.call-update
  11.5 0.0 all-gather.12.cloned.1.call-start
  11.5 17.0 %all-gather.10.cloned.1.call-done = f32[256,2048]{1,0:T(8,128)} async-done(((f32[128,2048]{1,0:T(8,128)}), f32[256,2048]{1,0:T(8,128)}) %all-gather.10.cloned.1.call-update) | async-done | bytes 2097168 | tf_op jit(solution)/shard_map/all_gather | solution.py:28
  28.6 0.0 all-gather.12.cloned.1.call-update
  28.6 0.0 all-gather.6.cloned.1.call-start
  28.6 2.1 reshape.12
  30.8 0.9 constant_dynamic-slice_fusion.1
  31.7 0.1 copy.16
  31.8 0.3 collective-permute-start.1
  32.1 0.0 copy-start.1
  32.1 0.0 copy-start.2
  32.1 0.1 copy.17
  32.2 0.8 collective-permute-start
  33.0 0.8 collective-permute-done.1
  33.8 0.0 collective-permute-done
  33.8 0.2 select_add_fusion.2
  34.0 1.0 pad_maximum_fusion
  35.0 0.0 all-gather.6.cloned.1.call-update
  35.0 0.0 all-gather.14.cloned.1.call-start
  35.1 114.8 %all-gather.12.cloned.1.call-done = f32[1024,2048]{1,0:T(8,128)} async-done(((f32[256,2048]{1,0:T(8,128)}), f32[1024,2048]{1,0:T(8,128)}) %all-gather.12.cloned.1.call-update) | async-done | bytes 8388624 | tf_op jit(solution)/shard_map/all_gather | solution.py:28
  149.9 0.0 all-gather.14.cloned.1.call-update
  149.9 0.0 all-gather.8.cloned.1.call-start
  150.0 39.1 %all-gather.6.cloned.1.call-done = f32[512,1024]{1,0:T(8,128)} async-done(((f32[256,1024]{1,0:T(8,128)}), f32[512,1024]{1,0:T(8,128)}) %all-gather.6.cloned.1.call-update) | async-done | bytes 2097168 | tf_op jit(solution)/shard_map/all_gather | solution.py:47
  189.1 0.0 all-gather.8.cloned.1.call-update
  189.1 0.0 copy-done.1
  189.1 0.0 copy-done.2
  189.1 0.2 fusion
  189.3 0.1 copy.10
  189.4 0.0 copy-done
  189.4 0.6 fusion.3
  189.9 0.0 copy-start.3
  190.0 201.3 %all-gather.14.cloned.1.call-done = f32[2048,2048]{1,0:T(8,128)} async-done(((f32[1024,2048]{1,0:T(8,128)}), f32[2048,2048]{1,0:T(8,128)}) %all-gather.14.cloned.1.call-update) | async-done | bytes 16777232 | tf_op jit(solution)/shard_map/all_gather | solution.py:28
  391.3 11.2 %fusion.2 = f32[2048,64]{0,1:T(8,128)S(1)} fusion(f32[2048,2048]{1,0:T(8,128)} %all-gather.14.cloned.1.call-done, f32[64,2048]{1,0:T(8,128)S(1)} %copy-done.1), kind=kOutput, calls=%fused_computation.26 | convolution fusion | flops 1610612736 | bytes 17825792 | tf_op jit(solution)/shard_map/dot_general | solution.py:55
  402.5 0.1 concatenate.31
  402.6 2.8 collective-permute-start.2
  405.4 23.8 %collective-permute-done.2 = f32[2050,64]{0,1:T(8,128)S(1)} collective-permute-done((f32[2050,64]{0,1:T(8,128)S(1)}, f32[2050,64]{0,1:T(8,128)S(1)}, u32[]{:S(2)}, u32[]{:S(2)}) %collective-permute-start.2) | collective-permute-done | bytes 524832 | tf_op jit(solution)/shard_map/ppermute | solution.py:64
  429.3 0.1 add.82
  429.3 0.1 collective-permute-start.3
  429.4 26.0 %collective-permute-done.3 = f32[2050,64]{0,1:T(8,128)S(1)} collective-permute-done((f32[2050,64]{0,1:T(8,128)S(1)}, f32[2050,64]{0,1:T(8,128)S(1)}, u32[]{:S(2)}, u32[]{:S(2)}) %collective-permute-start.3) | collective-permute-done | bytes 524832 | tf_op jit(solution)/shard_map/ppermute | solution.py:64
  455.4 0.1 add.83
  455.5 1.1 collective-permute-start.4
  456.6 0.0 copy-done.3
  456.6 12.5 %collective-permute-done.4 = f32[2050,64]{0,1:T(8,128)S(1)} collective-permute-done((f32[2050,64]{0,1:T(8,128)S(1)}, f32[2050,64]{0,1:T(8,128)S(1)}, u32[]{:S(2)}, u32[]{:S(2)}) %collective-permute-start.4) | collective-permute-done | bytes 524832 | tf_op jit(solution)/shard_map/ppermute | solution.py:64
  469.1 0.1 add.84
  469.2 0.2 slice_reduce_fusion
  469.4 0.1 fusion.1
  469.5 3.1 collective-permute-start.5
  472.6 0.8 collective-permute-done.5
  473.4 0.1 broadcast_select_fusion.1
  473.5 0.5 collective-permute-start.6
  474.1 2.3 collective-permute-done.6
  476.3 2.0 collective-permute-start.7
  478.4 1.9 collective-permute-done.7
  480.3 0.0 collective-permute-start.8
  480.3 18.3 %all-gather.8.cloned.1.call-done = f32[2048,1024]{1,0:T(8,128)} async-done(((f32[512,1024]{1,0:T(8,128)}), f32[2048,1024]{1,0:T(8,128)}) %all-gather.8.cloned.1.call-update) | async-done | bytes 8388624 | tf_op jit(solution)/shard_map/all_gather | solution.py:47
  498.6 33.8 %select_add_fusion = f32[1024,2048]{1,0:T(8,128)} fusion(f32[2048]{0:T(1024)S(1)} %copy-done.2, s32[2048]{0:T(1024)S(1)} %iota_add_fusion, s32[1024]{0:T(1024)S(1)} %iota_add_fusion.1, f32[2048,1024]{1,0:T(8,128)} %all-gather.8.cloned.1.call-done, f32[2048,2048]{1,0:T(8,128)} %all-gather.14.cloned.1.call-done), kind=kOutput, calls=%fused_computation.1 | convolution fusion | flops 25776095232 | bytes 33574912 | tf_op jit(solution)/shard_map/dot_general | solution.py:49
  532.4 0.0 collective-permute-done.8
  532.4 3.4 gather_fusion
  (8 shorter events, 0.1 us)
Async XLA Ops:
  7.2 182.2 %copy-start = (f32[2048]{0:T(1024)S(1)}, f32[2048]{0:T(1024)}, u32[]{:S(2)}) copy-start(f32[2048]{0:T(1024)} %param.11) | copy-start | bytes 24580
  7.2 21.4 %all-gather.10.cloned.1.call-start = ((), (), s32[]{:S(2)}) async-start(), calls=%async_computation.2 | async-start | bytes 3145728 | tf_op jit(solution)/shard_map/all_gather | solution.py:28
  11.5 138.4 %all-gather.12.cloned.1.call-start = ((), (), s32[]{:S(2)}) async-start(), calls=%async_computation.3 | async-start | bytes 10485760 | tf_op jit(solution)/shard_map/all_gather | solution.py:28
  28.6 160.5 %all-gather.6.cloned.1.call-start = ((), (), s32[]{:S(2)}) async-start(), calls=%async_computation | async-start | bytes 3145728 | tf_op jit(solution)/shard_map/all_gather | solution.py:47
  31.8 2.0 collective-permute-start.1
  32.1 157.0 %copy-start.1 = (f32[64,2048]{1,0:T(8,128)S(1)}, f32[64,2048]{1,0:T(8,128)}, u32[]{:S(2)}) copy-start(f32[64,2048]{1,0:T(8,128)} %param.9) | copy-start | bytes 1572868
  32.1 157.0 %copy-start.2 = (f32[2048]{0:T(1024)S(1)}, f32[2048]{0:T(1024)}, u32[]{:S(2)}) copy-start(f32[2048]{0:T(1024)} %param.8) | copy-start | bytes 24580
  32.2 1.6 collective-permute-start
  35.0 356.2 %all-gather.14.cloned.1.call-start = ((), (), s32[]{:S(2)}) async-start(), calls=%async_computation.4 | async-start | bytes 25165824 | tf_op jit(solution)/shard_map/all_gather | solution.py:28
  149.9 348.6 %all-gather.8.cloned.1.call-start = ((), (), s32[]{:S(2)}) async-start(), calls=%async_computation.1 | async-start | bytes 10485760 | tf_op jit(solution)/shard_map/all_gather | solution.py:47
  189.9 266.6 %copy-start.3 = (s32[512]{0:T(512)S(1)}, s32[512]{0:T(512)}, u32[]{:S(2)}) copy-start(s32[512]{0:T(512)} %param.10) | copy-start | bytes 6148
  402.6 26.6 %collective-permute-start.2 = (f32[2050,64]{0,1:T(8,128)S(1)}, f32[2050,64]{0,1:T(8,128)S(1)}, u32[]{:S(2)}, u32[]{:S(2)}) collective-permute-start(f32[2050,64]{0,1:T(8,128)S(1)} %concatenate.31), channel_id=1, source_target_pairs={{0,4},{1,5},{2,6},{3,7},{4,0},{5,1},{6,2},{7,3},{8,12},{9,13},{10,... | collective-permute-start | bytes 1574408 | tf_op jit(solution)/shard_map/ppermute | solution.py:64
  429.3 26.1 %collective-permute-start.3 = (f32[2050,64]{0,1:T(8,128)S(1)}, f32[2050,64]{0,1:T(8,128)S(1)}, u32[]{:S(2)}, u32[]{:S(2)}) collective-permute-start(f32[2050,64]{0,1:T(8,128)S(1)} %add.82), channel_id=1, source_target_pairs={{0,2},{1,3},{2,0},{3,1},{4,6},{5,7},{6,4},{7,5},{8,10},{9,11},{10,... | collective-permute-start | bytes 1574408 | tf_op jit(solution)/shard_map/ppermute | solution.py:64
  455.5 13.6 %collective-permute-start.4 = (f32[2050,64]{0,1:T(8,128)S(1)}, f32[2050,64]{0,1:T(8,128)S(1)}, u32[]{:S(2)}, u32[]{:S(2)}) collective-permute-start(f32[2050,64]{0,1:T(8,128)S(1)} %add.83), channel_id=1, source_target_pairs={{0,1},{1,0},{2,3},{3,2},{4,5},{5,4},{6,7},{7,6},{8,9},{9,8},{10,11... | collective-permute-start | bytes 1574408 | tf_op jit(solution)/shard_map/ppermute | solution.py:64
  469.5 3.9 collective-permute-start.5
  473.5 2.8 collective-permute-start.6
  476.3 3.9 collective-permute-start.7
  480.3 52.1 %collective-permute-start.8 = (f32[512]{0:T(512)S(1)}, f32[512]{0:T(512)S(1)}, u32[]{:S(2)}, u32[]{:S(2)}) collective-permute-start(f32[512]{0:T(512)S(1)} %maximum_select_fusion.1), channel_id=1, source_target_pairs={{0,64},{8,72},{16,80},{24,88},{32,96},{40,104},{48,112},{56,120},{... | collective-permute-start | bytes 6152 | tf_op jit(solution)/shard_map/ppermute | solution.py:75
Sparse Core Ops, SparseCore 0:
  11.6 16.9 all-gather.9
  30.2 119.6 all-gather.11
  152.1 36.9 all-gather.5
  190.6 200.6 all-gather.13
  392.8 105.7 all-gather.7
where the time goes:
time: 543 us; the launch traced here: 542 us
  waiting for transfers between devices  459 us (85%)
  matrix products  45.6 us (8%)
  between operations  14 us (3%)
  starting transfers between devices  10.9 us (2%)
  local copies, waits for them, and re-layouts  8.25 us (2%)
    all_gather x3, waiting for transfers between devices, body(): col_all = lax.all_gather(col_all, name, axis=0, tiled=True)  333 us
    ppermute x3, waiting for transfers between devices, body(): packed = packed + lax.ppermute(packed, COL, pairs)  62.4 us
    all_gather x2, waiting for transfers between devices, body(): row_all = lax.all_gather(row_all, name, axis=0, tiled=True)  57.4 us
    dot_general x1, matrix products, body(): lax.dot_general(row_all, col_all, contract, precision=high, preferred_ele...  33.8 us
    dot_general x1, matrix products, body(): lax.dot_general(col_all, items, (((1,), (1,)), ((), ())), precision=high,...  11.2 us
  transfers between devices with their start and end apart: 14, of which 12 were waited for; matrix products, arithmetic and copies ran while one was open for 9% of the time, Pallas kernels for 0%

commit v1 on v0

--- a/solution.py
+++ b/solution.py
@@ -44,7 +44,9 @@
     row_block = jnp.concatenate(ordered, axis=0)
     row_all = row_block
     for name in reversed(COL):
-        row_all = lax.all_gather(row_all, name, axis=0, tiled=True)
+        row_all = jnp.concatenate(
+            lax.all_to_all(jnp.stack([row_all] * lax.axis_size(name)), name, 0, 0), axis=0
+        )
     contract = (((0,), (0,)), ((), ()))
     tile = lax.dot_general(
         row_all, col_all, contract, precision=high, preferred_element_type=jnp.float32

time: 543 us -> 482 us (0.89)
  waiting for transfers between devices: 459 us -> 285 us
  blocking collectives: 0 us -> 91.9 us
  starting transfers between devices: 10.9 us -> 28.1 us
    all_gather x3, waiting for transfers between devices: 333 us -> 240 us  [body(): col_all = lax.all_gather(col_all, name, axis=0, tiled=True)]
    all_to_all x0 -> x1, blocking collectives: none -> 91.9 us  [body(): lax.all_to_all(jnp.stack([row_all] * lax.axis_size(name)), name, 0, 0)]
    all_gather x2 -> x0, waiting for transfers between devices: 57.4 us -> none  [body(): row_all = lax.all_gather(row_all, name, axis=0, tiled=True)]
    ppermute x3, waiting for transfers between devices: 62.4 us -> 38.6 us  [body(): packed = packed + lax.ppermute(packed, COL, pairs)]
    all_to_all x0 -> x1, starting transfers between devices: none -> 14.2 us  [body(): lax.all_to_all(jnp.stack([row_all] * lax.axis_size(name)), name, 0, 0)]
  transfers between devices with their start and end apart: 14 -> 13, of which waited for: 12 -> 10; matrix products, arithmetic and copies ran while one was open for 9% -> 11% of each run, Pallas kernels for 0% -> 0%
where the time goes in v1:
time: 482 us; the launch traced here: 480 us
  waiting for transfers between devices  285 us (59%)
  blocking collectives  91.9 us (19%)
  matrix products  45.7 us (9%)
  starting transfers between devices  28.1 us (6%)
  between operations  14 us (3%)
  local copies, waits for them, and re-layouts  11.5 us (2%)
    all_gather x3, waiting for transfers between devices, body(): col_all = lax.all_gather(col_all, name, axis=0, tiled=True)  240 us
    all_to_all x1, blocking collectives, body(): lax.all_to_all(jnp.stack([row_all] * lax.axis_size(name)), name, 0, 0)  91.9 us
    ppermute x3, waiting for transfers between devices, body(): packed = packed + lax.ppermute(packed, COL, pairs)  38.6 us
    dot_general x1, matrix products, body(): lax.dot_general(row_all, col_all, contract, precision=high, preferred_ele...  33.9 us
    all_to_all x1, starting transfers between devices, body(): lax.all_to_all(jnp.stack([row_all] * lax.axis_size(name)), name, 0, 0)  14.2 us
    dot_general x1, matrix products, body(): lax.dot_general(col_all, items, (((1,), (1,)), ((), ())), precision=high,...  11.3 us
  transfers between devices with their start and end apart: 13, of which 10 were waited for; matrix products, arithmetic and copies ran while one was open for 11% of the time, Pallas kernels for 0%

profile of v1, /device:TPU:1, one launch (start us, length us, event | category | flops | bytes accessed | tf_op | source)
XLA Modules:
  0.0 480.1 jit_solution(11619693049269498927)
XLA Ops:
  7.2 0.0 copy-start
  7.2 0.0 all-gather.4.cloned.1.call-start
  7.2 1.2 dynamic_slice.9
  8.5 0.6 iota_compare_fusion
  9.1 2.3 broadcast_select_fusion
  11.5 0.0 copy-start.2
  11.5 0.0 all-gather.4.cloned.1.call-update
  11.5 0.0 all-gather.6.cloned.1.call-start
  11.5 17.0 %all-gather.4.cloned.1.call-done = f32[256,2048]{1,0:T(8,128)} async-done(((f32[128,2048]{1,0:T(8,128)}), f32[256,2048]{1,0:T(8,128)}) %all-gather.4.cloned.1.call-update) | async-done | bytes 2097168 | tf_op jit(solution)/shard_map/all_gather | solution.py:28
  28.6 0.0 all-gather.6.cloned.1.call-update
  28.6 0.0 all-gather.8.cloned.1.call-start
  28.6 85.6 %all-gather.6.cloned.1.call-done = f32[1024,2048]{1,0:T(8,128)} async-done(((f32[256,2048]{1,0:T(8,128)}), f32[1024,2048]{1,0:T(8,128)}) %all-gather.6.cloned.1.call-update) | async-done | bytes 8388624 | tf_op jit(solution)/shard_map/all_gather | solution.py:28
  114.3 0.0 all-gather.8.cloned.1.call-update
  114.3 0.0 copy-done.2
  114.3 0.9 reshape.17
  115.2 0.9 constant_dynamic-slice_fusion.1
  116.1 0.1 copy.16
  116.2 0.8 collective-permute-start.1
  117.0 0.1 copy.17
  117.1 0.7 collective-permute-start
  117.8 0.7 collective-permute-done.1
  118.5 0.0 collective-permute-done
  118.5 0.2 select_add_fusion.2
  118.7 0.1 maximum_bitcast_fusion
  118.8 0.3 pad_maximum_fusion
  119.1 91.9 %all_to_all.10 = f32[2,256,1024]{2,1,0:T(8,128)S(1)} all-to-all(f32[2,256,1024]{2,1,0:T(8,128)S(1)} %pad_maximum_fusion), channel_id=1, replica_groups=mesh['zl'=2,'x'=4,'core'=2,'y'=4,'zh'=2] {'zh'}, dimensions={0} | all-to-all | bytes 4194304 | tf_op jit(solution)/shard_map/all_to_all | solution.py:48
  211.0 4.5 stack.12
  215.5 0.0 copy-start.3
  215.5 14.2 %all-to-all-start.1 = ((f32[4,512,1024]{2,1,0:T(8,128)}), f32[4,512,1024]{2,1,0:T(8,128)}, u32[]{:S(2)}, u32[]{:S(2)}) async-start(f32[4,512,1024]{2,1,0:T(8,128)} %stack.12), calls=%async_computation.1 | async-start | bytes 16777216 | tf_op jit(solution)/shard_map/all_to_all | solution.py:48
  229.7 0.0 copy-done.3
  229.7 0.0 copy-done.4
  229.7 0.2 fusion
  229.9 0.1 copy.10
  230.0 0.0 copy-done
  230.0 0.6 fusion.3
  230.5 0.0 copy-start.5
  230.6 137.8 %all-gather.8.cloned.1.call-done = f32[2048,2048]{1,0:T(8,128)} async-done(((f32[1024,2048]{1,0:T(8,128)}), f32[2048,2048]{1,0:T(8,128)}) %all-gather.8.cloned.1.call-update) | async-done | bytes 16777232 | tf_op jit(solution)/shard_map/all_gather | solution.py:28
  368.3 11.3 %fusion.2 = f32[2048,64]{0,1:T(8,128)S(1)} fusion(f32[2048,2048]{1,0:T(8,128)} %all-gather.8.cloned.1.call-done, f32[64,2048]{1,0:T(8,128)S(1)} %copy-done.3), kind=kOutput, calls=%fused_computation.27 | convolution fusion | flops 1610612736 | bytes 17825792 | tf_op jit(solution)/shard_map/dot_general | solution.py:57
  379.6 0.1 concatenate.31
  379.7 3.8 collective-permute-start.2
  383.5 12.6 %collective-permute-done.2 = f32[2050,64]{0,1:T(8,128)S(1)} collective-permute-done((f32[2050,64]{0,1:T(8,128)S(1)}, f32[2050,64]{0,1:T(8,128)S(1)}, u32[]{:S(2)}, u32[]{:S(2)}) %collective-permute-start.2) | collective-permute-done | bytes 524832 | tf_op jit(solution)/shard_map/ppermute | solution.py:66
  396.1 0.1 add.82
  396.2 2.5 collective-permute-start.3
  398.7 12.0 %collective-permute-done.3 = f32[2050,64]{0,1:T(8,128)S(1)} collective-permute-done((f32[2050,64]{0,1:T(8,128)S(1)}, f32[2050,64]{0,1:T(8,128)S(1)}, u32[]{:S(2)}, u32[]{:S(2)}) %collective-permute-start.3) | collective-permute-done | bytes 524832 | tf_op jit(solution)/shard_map/ppermute | solution.py:66
  410.7 0.1 add.83
  410.7 0.1 collective-permute-start.4
  410.8 0.0 copy-done.5
  410.8 14.0 %collective-permute-done.4 = f32[2050,64]{0,1:T(8,128)S(1)} collective-permute-done((f32[2050,64]{0,1:T(8,128)S(1)}, f32[2050,64]{0,1:T(8,128)S(1)}, u32[]{:S(2)}, u32[]{:S(2)}) %collective-permute-start.4) | collective-permute-done | bytes 524832 | tf_op jit(solution)/shard_map/ppermute | solution.py:66
  424.8 0.1 add.84
  424.9 0.2 slice_reduce_fusion
  425.1 0.1 fusion.1
  425.2 2.6 collective-permute-start.5
  427.8 0.8 collective-permute-done.5
  428.6 0.1 broadcast_select_fusion.1
  428.7 0.3 collective-permute-start.6
  429.1 2.1 collective-permute-done.6
  431.1 1.8 collective-permute-start.7
  433.0 2.1 collective-permute-done.7
  435.1 1.2 collective-permute-start.8
  436.2 0.0 all-to-all-done.1
  436.2 33.9 %select_add_fusion = f32[1024,2048]{1,0:T(8,128)} fusion(f32[2048]{0:T(1024)S(1)} %copy-done.4, s32[2048]{0:T(1024)S(1)} %iota_add_fusion, s32[1024]{0:T(1024)S(1)} %iota_add_fusion.1, f32[2048,1024]{1,0:T(8,128)} %bitcast.3, f32[2048,2048]{1,0:T(8,128)} %all-gather.8.cloned.1.call-done), kind=kOutput, calls=%fused_computation.1 | convolution fusion | flops 25776095232 | bytes 33574912 | tf_op jit(solution)/shard_map/dot_general | solution.py:51
  470.1 0.0 collective-permute-done.8
  470.1 3.4 gather_fusion
  473.5 0.0 copy-done.1
  (10 shorter events, 0.1 us)
Async XLA Ops:
  7.2 222.8 %copy-start = (f32[2048]{0:T(1024)S(1)}, f32[2048]{0:T(1024)}, u32[]{:S(2)}) copy-start(f32[2048]{0:T(1024)} %param.11) | copy-start | bytes 24580
  7.2 21.4 %all-gather.4.cloned.1.call-start = ((), (), s32[]{:S(2)}) async-start(), calls=%async_computation.2 | async-start | bytes 3145728 | tf_op jit(solution)/shard_map/all_gather | solution.py:28
  11.5 102.8 %copy-start.2 = (f32[128,2048]{1,0:T(8,128)S(1)}, f32[128,2048]{1,0:T(8,128)}, u32[]{:S(2)}) copy-start(f32[128,2048]{1,0:T(8,128)} %broadcast_select_fusion) | copy-start | bytes 3145732
  11.5 102.8 %all-gather.6.cloned.1.call-start = ((), (), s32[]{:S(2)}) async-start(), calls=%async_computation.3 | async-start | bytes 10485760 | tf_op jit(solution)/shard_map/all_gather | solution.py:28
  28.6 339.7 %all-gather.8.cloned.1.call-start = ((), (), s32[]{:S(2)}) async-start(), calls=%async_computation.4 | async-start | bytes 25165824 | tf_op jit(solution)/shard_map/all_gather | solution.py:28
  116.2 2.3 collective-permute-start.1
  117.1 1.4 collective-permute-start
  215.5 14.2 %copy-start.3 = (f32[64,2048]{1,0:T(8,128)S(1)}, f32[64,2048]{1,0:T(8,128)}, u32[]{:S(2)}) copy-start(f32[64,2048]{1,0:T(8,128)} %param.9) | copy-start | bytes 1572868
  215.5 14.2 %copy-start.4 = (f32[2048]{0:T(1024)S(1)}, f32[2048]{0:T(1024)}, u32[]{:S(2)}) copy-start(f32[2048]{0:T(1024)} %param.8) | copy-start | bytes 24580
  215.5 220.7 %all-to-all-start.1 = ((f32[4,512,1024]{2,1,0:T(8,128)}), f32[4,512,1024]{2,1,0:T(8,128)}, u32[]{:S(2)}, u32[]{:S(2)}) async-start(f32[4,512,1024]{2,1,0:T(8,128)} %stack.12), calls=%async_computation.1 | async-start | bytes 16777216 | tf_op jit(solution)/shard_map/all_to_all | solution.py:48
  230.5 180.3 %copy-start.5 = (s32[512]{0:T(512)S(1)}, s32[512]{0:T(512)}, u32[]{:S(2)}) copy-start(s32[512]{0:T(512)} %param.10) | copy-start | bytes 6148
  379.7 16.4 %collective-permute-start.2 = (f32[2050,64]{0,1:T(8,128)S(1)}, f32[2050,64]{0,1:T(8,128)S(1)}, u32[]{:S(2)}, u32[]{:S(2)}) collective-permute-start(f32[2050,64]{0,1:T(8,128)S(1)} %concatenate.31), channel_id=1, source_target_pairs={{0,4},{1,5},{2,6},{3,7},{4,0},{5,1},{6,2},{7,3},{8,12},{9,13},{10,... | collective-permute-start | bytes 1574408 | tf_op jit(solution)/shard_map/ppermute | solution.py:66
  396.2 14.5 %collective-permute-start.3 = (f32[2050,64]{0,1:T(8,128)S(1)}, f32[2050,64]{0,1:T(8,128)S(1)}, u32[]{:S(2)}, u32[]{:S(2)}) collective-permute-start(f32[2050,64]{0,1:T(8,128)S(1)} %add.82), channel_id=1, source_target_pairs={{0,2},{1,3},{2,0},{3,1},{4,6},{5,7},{6,4},{7,5},{8,10},{9,11},{10,... | collective-permute-start | bytes 1574408 | tf_op jit(solution)/shard_map/ppermute | solution.py:66
  410.7 14.1 %collective-permute-start.4 = (f32[2050,64]{0,1:T(8,128)S(1)}, f32[2050,64]{0,1:T(8,128)S(1)}, u32[]{:S(2)}, u32[]{:S(2)}) collective-permute-start(f32[2050,64]{0,1:T(8,128)S(1)} %add.83), channel_id=1, source_target_pairs={{0,1},{1,0},{2,3},{3,2},{4,5},{5,4},{6,7},{7,6},{8,9},{9,8},{10,11... | collective-permute-start | bytes 1574408 | tf_op jit(solution)/shard_map/ppermute | solution.py:66
  425.2 3.4 collective-permute-start.5
  428.7 2.4 collective-permute-start.6
  431.1 3.9 collective-permute-start.7
  435.1 35.0 %collective-permute-start.8 = (f32[512]{0:T(512)S(1)}, f32[512]{0:T(512)S(1)}, u32[]{:S(2)}, u32[]{:S(2)}) collective-permute-start(f32[512]{0:T(512)S(1)} %maximum_select_fusion.1), channel_id=1, source_target_pairs={{0,64},{8,72},{16,80},{24,88},{32,96},{40,104},{48,112},{56,120},{... | collective-permute-start | bytes 6152 | tf_op jit(solution)/shard_map/ppermute | solution.py:77
  436.2 37.3 %copy-start.1 = (f32[2048]{0:T(1024)S(1)}, f32[2048]{0:T(1024)}, u32[]{:S(2)}) copy-start(f32[2048]{0:T(1024)} %param.11) | copy-start | bytes 24580
Sparse Core Ops, SparseCore 0:
  11.6 16.9 all-gather.3
  30.2 83.9 all-gather.5
  115.9 252.3 all-gather.7
